TPU v7x, 512 devices: a whole 4x8x8 slice. The times are simulated.
512 devices in a mesh: section: 2 (over z_lo), tensor: 4 (over x), seq: 64 (over y, z_hi, core).
Axes of the slice: x: 4, y: 8, z: 8 (z_hi: 4, z_lo: 2; z = z_hi * 2 + z_lo), core: 2. Of those that a mesh axis runs over, the one named last changes fastest.
Arguments:
- tokens: bfloat16 [16384, 2560], P('seq', ('section', 'tensor')), may hold values from -6 to 6
- w_query: bfloat16 [2560, 2048], P(None, ('section', 'tensor')), may hold values from -0.125 to 0.125
- w_keyval: bfloat16 [2560, 2048], P(None, ('section', 'tensor')), may hold values from -0.125 to 0.125
- w_out: bfloat16 [2048, 2560], P(('section', 'tensor')), may hold values from -0.125 to 0.125
- w_gateup: bfloat16 [2560, 2, 5120], P('seq', None, ('section', 'tensor')), may hold values from -0.125 to 0.125
- attn_gain: float32 [2560], replicated, may hold values from 0.1 to 1.9
- post_gain: float32 [2560], replicated, may hold values from 0.1 to 1.9
- mlp_gain: float32 [2560], replicated, may hold values from 0.1 to 1.9
- query_gain: float32 [256], replicated, may hold values from 0.7 to 6.5
- key_gain: float32 [256], replicated, may hold values from 0.7 to 6.5
- prompt_lengths: int32 [8], replicated, may hold values from 1 to 4096, as said below
- page_slots: int32 [128], P('seq'), may hold values from 0 to 1, as said below
Outputs:
- hidden: bfloat16 [16384, 5120], P('seq', ('section', 'tensor'))
- page_cache: bfloat16 [128, 128, 2048], P('seq', None, ('section', 'tensor'))
Inputs may be any that keep to these rules, and one draw needn't show every extreme that they name: `prompt_lengths`: each prompt has at least one token; they sum to 16384; one prompt has exactly 4096 tokens and begins strictly inside a token block. `page_slots`: within each aligned group of 2 pages (the pages of one token block) the slots are a permutation of 0 to 1.
All inputs are finite; a program needn't handle non-finite values.
Results may differ from a plain program's by a relative error of at most 0.01.
The roundings to bfloat16 on the way count: a program that leaves them out, or rounds other values in their place, can miss the bound.
Values may be sent and summed in bfloat16 or wider, within the bound.
No kernel may reach another device: no remote copies, remote signals or barrier semaphores. Data moves between devices by JAX's collectives and lax.ppermute only.
A program may use at most 64 MiB of HBM per device.

v0:
```python
import jax
import jax.numpy as jnp
from jax import lax
from jax.sharding import PartitionSpec as P

REACH = 16
NORM_EPS = 1e-06
ROPE_BASE = 1000000.0
ROPE_FACTOR = 8.0


def swapped(value, axis, bit):
    mask = 2**bit
    pairs = [(source, source ^ mask) for source in range(lax.axis_size(axis))]
    return lax.ppermute(value, axis, pairs)


def shifted(block, axis, distance):
    devices = range(lax.axis_size(axis))
    route = [(i - distance, i) for i in devices if i - distance in devices]
    return lax.ppermute(block, axis, route)


def rms_norm(values, weights):
    values = values.astype(jnp.float32)
    inverse = lax.rsqrt(jnp.mean(values * values, axis=-1, keepdims=True) + NORM_EPS)
    return values * inverse * weights


def angle_tables(position, head_width):
    halfway = head_width // 2
    exponent = jnp.arange(halfway, dtype=jnp.float32) * (2.0 / head_width)
    frequency = ROPE_BASE ** (-exponent)
    angles = (position.astype(jnp.float32) / ROPE_FACTOR)[:, None] * frequency[None, :]
    return (jnp.cos(angles), jnp.sin(angles))


def rotary(values, cosine_table, sine_table):
    halfway = values.shape[-1] // 2
    lower_half = values[..., :halfway]
    upper_half = values[..., halfway:]
    return jnp.concatenate(
        [
            lower_half * cosine_table - upper_half * sine_table,
            upper_half * cosine_table + lower_half * sine_table,
        ],
        axis=-1,
    )


def local(
    tokens,
    w_query,
    w_keyval,
    w_out,
    w_gateup,
    attn_gain,
    post_gain,
    mlp_gain,
    query_gain,
    key_gain,
    prompt_lengths,
    page_slots,
):
    row_count = tokens.shape[0]
    head_width = w_query.shape[1]
    halfway = head_width // 2
    unit_count = w_gateup.shape[2]
    span_blocks = min(REACH, lax.axis_size("seq") // 2)
    features = lax.all_gather(tokens, ("section", "tensor"), axis=1, tiled=True)
    first_row = lax.axis_index("seq") * row_count
    prompt_ends = jnp.cumsum(prompt_lengths)
    prompt_starts = prompt_ends - prompt_lengths
    query_index = first_row + jnp.arange(row_count, dtype=jnp.int32)
    query_segment = jnp.sum(
        (prompt_ends[None, :] <= query_index[:, None]).astype(jnp.int32), axis=1
    )
    chosen = query_segment[:, None] == jnp.arange(prompt_ends.shape[0], dtype=jnp.int32)[None, :]
    query_position = query_index - jnp.sum(jnp.where(chosen, prompt_starts[None, :], 0), axis=1)
    cosine_table, sine_table = angle_tables(query_position, head_width)
    normed = rms_norm(features, attn_gain).astype(jnp.bfloat16)
    queries = jnp.dot(normed, w_query, preferred_element_type=jnp.float32)
    queries = rotary(rms_norm(queries, query_gain), cosine_table, sine_table).astype(jnp.bfloat16)
    own_half = jnp.dot(normed, w_keyval, preferred_element_type=jnp.float32).astype(jnp.bfloat16)
    other_half = swapped(own_half, "tensor", 0)
    is_lower = lax.axis_index("tensor") % 2 == 0
    lower_part = jnp.where(is_lower, own_half, other_half)
    upper_part = jnp.where(is_lower, other_half, own_half)
    raw_keys = jnp.concatenate([lower_part[:, :halfway], upper_part[:, :halfway]], axis=1)
    values_full = jnp.concatenate([lower_part[:, halfway:], upper_part[:, halfway:]], axis=1)
    keys_full = rotary(rms_norm(raw_keys, key_gain), cosine_table, sine_table).astype(jnp.bfloat16)
    own_keys = jnp.where(is_lower, keys_full[:, :halfway], keys_full[:, halfway:])
    page_rows = jnp.concatenate([own_keys, own_half[:, halfway:]], axis=1)
    pages_here = page_slots.shape[0]
    page_rows = page_rows.reshape(pages_here, row_count // pages_here, head_width)
    page_cache = jnp.zeros_like(page_rows).at[page_slots].set(page_rows)
    key_block = jnp.stack([keys_full, values_full])
    received = [key_block]
    for distance in range(1, span_blocks + 1):
        received.append(shifted(key_block, "seq", distance))
    window_stack = jnp.stack(received)
    all_keys = window_stack[:, 0].reshape(-1, head_width)
    all_values = window_stack[:, 1].reshape(-1, head_width)
    offsets = (jnp.arange(span_blocks + 1, dtype=jnp.int32) * row_count)[:, None]
    key_index = (first_row - offsets + jnp.arange(row_count, dtype=jnp.int32)[None, :]).reshape(-1)
    key_segment = jnp.sum((prompt_ends[None, :] <= key_index[:, None]).astype(jnp.int32), axis=1)
    key_segment = jnp.where(key_index >= 0, key_segment, -1)
    allowed = (key_segment[None, :] == query_segment[:, None]) & (
        key_index[None, :] <= query_index[:, None]
    )
    scores = lax.dot_general(
        queries, all_keys, (((1,), (1,)), ((), ())), preferred_element_type=jnp.float32
    ) * head_width ** (-0.5)
    scores = jnp.where(allowed, scores, -jnp.inf)
    row_max = jnp.max(scores, axis=1, keepdims=True)
    exponent_terms = jnp.exp(scores - row_max)
    weights_low = (exponent_terms / jnp.sum(exponent_terms, axis=1, keepdims=True)).astype(
        jnp.bfloat16
    )
    attention_out = jnp.dot(weights_low, all_values, preferred_element_type=jnp.float32).astype(
        jnp.bfloat16
    )
    head_terms = jnp.dot(attention_out, w_out, preferred_element_type=jnp.float32)
    attended = lax.psum(head_terms, ("section", "tensor"))
    residual = features.astype(jnp.float32) + rms_norm(attended, post_gain)
    ffn_input = rms_norm(residual, mlp_gain).astype(jnp.bfloat16)
    row_piece = lax.all_gather(w_gateup, "seq", axis=0, tiled=True)
    piece_rows = row_piece.shape[0]
    projected = jnp.dot(
        ffn_input, row_piece.reshape(piece_rows, 2 * unit_count), preferred_element_type=jnp.float32
    )
    hidden = (
        jax.nn.gelu(projected[:, :unit_count], approximate=True) * projected[:, unit_count:]
    ).astype(jnp.bfloat16)
    return (hidden, page_cache)


def solution(mesh):
    return jax.shard_map(
        local,
        mesh=mesh,
        in_specs=(
            P("seq", ("section", "tensor")),
            P(None, ("section", "tensor")),
            P(None, ("section", "tensor")),
            P(("section", "tensor"), None),
            P("seq", None, ("section", "tensor")),
            P(),
            P(),
            P(),
            P(),
            P(),
            P(),
            P("seq"),
        ),
        out_specs=(P("seq", ("section", "tensor")), P("seq", None, ("section", "tensor"))),
        check_vma=False,
    )
```

profile of v0, /device:TPU:8, one launch (start us, length us, event | category | flops | bytes accessed | tf_op | source)
XLA Modules:
  0.0 404.8 jit_solution(14164455643297318080)
XLA Ops:
  8.1 0.7 all-gather.3.cloned.1.call-update
  8.8 0.8 reduce-window.8
  9.8 0.7 bitcast_subtract_fusion
  10.6 0.1 convert_reduce_fusion
  10.7 49.9 %all-gather.3.cloned.1.call-done = bf16[256,2560]{0,1:T(8,128)(2,1)} async-done(((bf16[256,320]{0,1:T(8,128)(2,1)}), bf16[256,2560]{0,1:T(8,128)(2,1)}) %all-gather.3.cloned.1.call-update) | async-done | bytes 1310736 | tf_op jit(solution)/shard_map/all_gather | solution.py:70
  60.6 1.6 copy.24
  62.2 0.3 fusion.2
  62.6 2.1 convolution_convert_fusion
  64.7 1.9 collective-permute-start
  66.7 0.8 multiply_reduce_fusion.2
  67.6 4.0 collective-permute-done
  71.8 0.6 broadcast_select_fusion.2
  72.5 1.9 collective-permute-start.1
  74.4 0.6 fusion.36
  75.0 4.6 %collective-permute-start.2 = (bf16[2,256,256]{1,2,0:T(8,128)(2,1)S(1)}, bf16[2,256,256]{1,2,0:T(8,128)(2,1)S(1)}, u32[]{:S(2)}, u32[]{:S(2)}) collective-permute-start(bf16[2,256,256]{1,2,0:T(8,128)(2,1)S(1)} %pad_maximum_fusion), channel_id=1, source_target_pairs={{0,2},{1,3},{2,4},{3,5},{4,6},{5,7},{6,8},{7,9},{8,10},{9,11},{10,... | collective-permute-start | bytes 786440 | tf_op jit(solution)/shard_map/ppermute | solution.py:21
  79.6 5.3 %collective-permute-start.3 = (bf16[2,256,256]{1,2,0:T(8,128)(2,1)S(1)}, bf16[2,256,256]{1,2,0:T(8,128)(2,1)S(1)}, u32[]{:S(2)}, u32[]{:S(2)}) collective-permute-start(bf16[2,256,256]{1,2,0:T(8,128)(2,1)S(1)} %pad_maximum_fusion), channel_id=1, source_target_pairs={{0,3},{1,4},{2,5},{3,6},{4,7},{5,8},{6,9},{7,10},{8,11},{9,12},{10... | collective-permute-start | bytes 786440 | tf_op jit(solution)/shard_map/ppermute | solution.py:21
  84.9 5.4 %collective-permute-start.4 = (bf16[2,256,256]{1,2,0:T(8,128)(2,1)S(1)}, bf16[2,256,256]{1,2,0:T(8,128)(2,1)S(1)}, u32[]{:S(2)}, u32[]{:S(2)}) collective-permute-start(bf16[2,256,256]{1,2,0:T(8,128)(2,1)S(1)} %pad_maximum_fusion), channel_id=1, source_target_pairs={{0,4},{1,5},{2,6},{3,7},{4,8},{5,9},{6,10},{7,11},{8,12},{9,13},{1... | collective-permute-start | bytes 786440 | tf_op jit(solution)/shard_map/ppermute | solution.py:21
  90.3 4.8 %collective-permute-start.5 = (bf16[2,256,256]{1,2,0:T(8,128)(2,1)S(1)}, bf16[2,256,256]{1,2,0:T(8,128)(2,1)S(1)}, u32[]{:S(2)}, u32[]{:S(2)}) collective-permute-start(bf16[2,256,256]{1,2,0:T(8,128)(2,1)S(1)} %pad_maximum_fusion), channel_id=1, source_target_pairs={{0,5},{1,6},{2,7},{3,8},{4,9},{5,10},{6,11},{7,12},{8,13},{9,14},{... | collective-permute-start | bytes 786440 | tf_op jit(solution)/shard_map/ppermute | solution.py:21
  95.1 6.0 %collective-permute-start.6 = (bf16[2,256,256]{1,2,0:T(8,128)(2,1)S(1)}, bf16[2,256,256]{1,2,0:T(8,128)(2,1)S(1)}, u32[]{:S(2)}, u32[]{:S(2)}) collective-permute-start(bf16[2,256,256]{1,2,0:T(8,128)(2,1)S(1)} %pad_maximum_fusion), channel_id=1, source_target_pairs={{0,6},{1,7},{2,8},{3,9},{4,10},{5,11},{6,12},{7,13},{8,14},{9,15},... | collective-permute-start | bytes 786440 | tf_op jit(solution)/shard_map/ppermute | solution.py:21
  101.2 18.7 %collective-permute-start.7 = (bf16[2,256,256]{1,2,0:T(8,128)(2,1)S(1)}, bf16[2,256,256]{1,2,0:T(8,128)(2,1)S(1)}, u32[]{:S(2)}, u32[]{:S(2)}) collective-permute-start(bf16[2,256,256]{1,2,0:T(8,128)(2,1)S(1)} %pad_maximum_fusion), channel_id=1, source_target_pairs={{0,7},{1,8},{2,9},{3,10},{4,11},{5,12},{6,13},{7,14},{8,15},{9,16}... | collective-permute-start | bytes 786440 | tf_op jit(solution)/shard_map/ppermute | solution.py:21
  120.0 3.4 collective-permute-start.8
  123.4 1.3 collective-permute-start.9
  124.8 5.5 %collective-permute-start.10 = (bf16[2,256,256]{1,2,0:T(8,128)(2,1)S(1)}, bf16[2,256,256]{1,2,0:T(8,128)(2,1)S(1)}, u32[]{:S(2)}, u32[]{:S(2)}) collective-permute-start(bf16[2,256,256]{1,2,0:T(8,128)(2,1)S(1)} %pad_maximum_fusion), channel_id=1, source_target_pairs={{0,10},{1,11},{2,12},{3,13},{4,14},{5,15},{6,16},{7,17},{8,18},{9,... | collective-permute-start | bytes 786440 | tf_op jit(solution)/shard_map/ppermute | solution.py:21
  130.3 16.4 %collective-permute-start.11 = (bf16[2,256,256]{1,2,0:T(8,128)(2,1)S(1)}, bf16[2,256,256]{1,2,0:T(8,128)(2,1)S(1)}, u32[]{:S(2)}, u32[]{:S(2)}) collective-permute-start(bf16[2,256,256]{1,2,0:T(8,128)(2,1)S(1)} %pad_maximum_fusion), channel_id=1, source_target_pairs={{0,11},{1,12},{2,13},{3,14},{4,15},{5,16},{6,17},{7,18},{8,19},{9,... | collective-permute-start | bytes 786440 | tf_op jit(solution)/shard_map/ppermute | solution.py:21
  146.7 2.8 collective-permute-start.12
  149.6 4.5 %collective-permute-start.13 = (bf16[2,256,256]{1,2,0:T(8,128)(2,1)S(1)}, bf16[2,256,256]{1,2,0:T(8,128)(2,1)S(1)}, u32[]{:S(2)}, u32[]{:S(2)}) collective-permute-start(bf16[2,256,256]{1,2,0:T(8,128)(2,1)S(1)} %pad_maximum_fusion), channel_id=1, source_target_pairs={{0,13},{1,14},{2,15},{3,16},{4,17},{5,18},{6,19},{7,20},{8,21},{9,... | collective-permute-start | bytes 786440 | tf_op jit(solution)/shard_map/ppermute | solution.py:21
  154.1 5.3 %collective-permute-start.14 = (bf16[2,256,256]{1,2,0:T(8,128)(2,1)S(1)}, bf16[2,256,256]{1,2,0:T(8,128)(2,1)S(1)}, u32[]{:S(2)}, u32[]{:S(2)}) collective-permute-start(bf16[2,256,256]{1,2,0:T(8,128)(2,1)S(1)} %pad_maximum_fusion), channel_id=1, source_target_pairs={{0,14},{1,15},{2,16},{3,17},{4,18},{5,19},{6,20},{7,21},{8,22},{9,... | collective-permute-start | bytes 786440 | tf_op jit(solution)/shard_map/ppermute | solution.py:21
  159.5 13.2 %collective-permute-start.15 = (bf16[2,256,256]{1,2,0:T(8,128)(2,1)S(1)}, bf16[2,256,256]{1,2,0:T(8,128)(2,1)S(1)}, u32[]{:S(2)}, u32[]{:S(2)}) collective-permute-start(bf16[2,256,256]{1,2,0:T(8,128)(2,1)S(1)} %pad_maximum_fusion), channel_id=1, source_target_pairs={{0,15},{1,16},{2,17},{3,18},{4,19},{5,20},{6,21},{7,22},{8,23},{9,... | collective-permute-start | bytes 786440 | tf_op jit(solution)/shard_map/ppermute | solution.py:21
  172.8 30.3 %collective-permute-start.16 = (bf16[2,256,256]{1,2,0:T(8,128)(2,1)S(1)}, bf16[2,256,256]{1,2,0:T(8,128)(2,1)S(1)}, u32[]{:S(2)}, u32[]{:S(2)}) collective-permute-start(bf16[2,256,256]{1,2,0:T(8,128)(2,1)S(1)} %pad_maximum_fusion), channel_id=1, source_target_pairs={{0,16},{1,17},{2,18},{3,19},{4,20},{5,21},{6,22},{7,23},{8,24},{9,... | collective-permute-start | bytes 786440 | tf_op jit(solution)/shard_map/ppermute | solution.py:21
  203.2 7.7 %collective-permute-done.15 = bf16[2,256,256]{1,2,0:T(8,128)(2,1)S(1)} collective-permute-done((bf16[2,256,256]{1,2,0:T(8,128)(2,1)S(1)}, bf16[2,256,256]{1,2,0:T(8,128)(2,1)S(1)}, u32[]{:S(2)}, u32[]{:S(2)}) %collective-permute-start.15) | collective-permute-done | bytes 262176 | tf_op jit(solution)/shard_map/ppermute | solution.py:21
  210.9 5.6 %collective-permute-done.16 = bf16[2,256,256]{1,2,0:T(8,128)(2,1)S(1)} collective-permute-done((bf16[2,256,256]{1,2,0:T(8,128)(2,1)S(1)}, bf16[2,256,256]{1,2,0:T(8,128)(2,1)S(1)}, u32[]{:S(2)}, u32[]{:S(2)}) %collective-permute-start.16) | collective-permute-done | bytes 262176 | tf_op jit(solution)/shard_map/ppermute | solution.py:21
  216.5 2.3 fusion.49
  218.9 4.1 %copy.25 = bf16[17,1,256,256]{3,2,0,1:T(8,128)(2,1)} copy(bf16[17,1,256,256]{2,3,1,0:T(8,128)(2,1)} %get-tuple-element.5) | data formatting | bytes 4456448 | tf_op jit(solution)/shard_map/slice | solution.py:102
  223.0 4.1 %copy.26 = bf16[17,1,256,256]{3,2,0,1:T(8,128)(2,1)} copy(bf16[17,1,256,256]{2,3,1,0:T(8,128)(2,1)} %get-tuple-element.6) | data formatting | bytes 4456448 | tf_op jit(solution)/shard_map/slice | solution.py:103
  227.1 3.3 fusion.52
  230.4 2.0 copy-done.3
  232.4 0.7 fusion.1
  233.2 6.4 %fusion.12 = f32[256,2560]{1,0:T(8,128)} fusion(bf16[256,2560]{1,0:T(8,128)(2,1)S(1)} %copy-done, bf16[4352,256]{1,0:T(8,128)(2,1)} %bitcast.54, f32[256,4352]{1,0:T(8,128)} %copy-done.3, f32[256]{0:T(256)S(1)} %fusion.1, f32[256]{0:T(256)S(1)} %get-tuple-element.17), kind=kOutput, calls=%fused_computation.23 | convolution fusion | flops 909377536 | bytes 10618880 | tf_op jit(solution)/shard_map/dot_general | solution.py:123
  239.6 0.2 all-gather.5.cloned.1.call-start
  239.9 0.3 all-gather.5.cloned.1.call-update
  240.4 0.6 scatter_fusion
  241.1 145.7 %all-reduce.2.cloned.1.call-done = f32[256,2560]{1,0:T(8,128)} async-done(((f32[256,2560]{1,0:T(8,128)}), f32[256,2560]{1,0:T(8,128)}) %all-reduce.2.cloned.1.call-update) | async-done | bytes 2621456 | tf_op jit(solution)/shard_map/psum | solution.py:124
  386.7 2.1 multiply_reduce_fusion.1
  388.9 0.4 copy-done.1
  389.3 0.7 multiply_reduce_fusion
  390.0 4.1 %copy.29 = bf16[320,8,2,640]{3,1,2,0:T(8,128)(2,1)S(1)} copy(bf16[320,8,2,640]{3,2,1,0:T(2,128)(2,1)} %bitcast.52) | data formatting | bytes 13107200
  394.2 2.2 fusion.6
  396.4 1.0 fusion.21
  (83 shorter events, 1.4 us)
Async XLA Ops:
  8.0 225.2 %copy-start = (bf16[256,2560]{1,0:T(8,128)(2,1)S(1)}, bf16[256,2560]{1,0:T(8,128)(2,1)}, u32[]{:S(2)}) copy-start(bf16[256,2560]{1,0:T(8,128)(2,1)} %param.15) | copy-start | bytes 3932164
  8.0 54.5 %copy-start.9 = (f32[2560]{0:T(1024)S(1)}, f32[2560]{0:T(1024)}, u32[]{:S(2)}) copy-start(f32[2560]{0:T(1024)} %param.17) | copy-start | bytes 30724
  8.0 52.6 %all-gather.3.cloned.1.call-start = ((), (), s32[]{:S(2)}) async-start(), calls=%async_computation | async-start | bytes 1474560 | tf_op jit(solution)/shard_map/all_gather | solution.py:70
  8.8 378.0 %all-reduce.2.cloned.1.call-start = ((), (), s32[]{:S(2)}) async-start(), calls=%async_computation.1 | async-start | bytes 5242880 | tf_op jit(solution)/shard_map/psum | solution.py:124
  62.2 4.5 %copy-start.8 = (bf16[2560,256]{1,0:T(8,128)(2,1)S(1)}, bf16[2560,256]{1,0:T(8,128)(2,1)}, u32[]{:S(2)}) copy-start(bf16[2560,256]{1,0:T(8,128)(2,1)} %param.13) | copy-start | bytes 3932164
  64.7 2.8 copy-start.6
  64.7 7.0 %copy-start.7 = (f32[256]{0:T(256)S(1)}, f32[256]{0:T(256)}, u32[]{:S(2)}) copy-start(f32[256]{0:T(256)} %param.21) | copy-start | bytes 3076
  64.7 6.9 %collective-permute-start = (bf16[256,256]{0,1:T(8,128)(2,1)S(1)}, bf16[256,256]{0,1:T(8,128)(2,1)S(1)}, u32[]{:S(2)}, u32[]{:S(2)}) collective-permute-start(bf16[256,256]{0,1:T(8,128)(2,1)S(1)} %convolution_convert_fusion), channel_id=1, source_target_pairs={{0,64},{64,0},{128,192},{192,128},{1,65},{65,1},{129,193},{193,129... | collective-permute-start | bytes 393224 | tf_op jit(solution)/shard_map/ppermute | solution.py:15
  72.5 22.6 %collective-permute-start.1 = (bf16[2,256,256]{1,2,0:T(8,128)(2,1)S(1)}, bf16[2,256,256]{1,2,0:T(8,128)(2,1)S(1)}, u32[]{:S(2)}, u32[]{:S(2)}) collective-permute-start(bf16[2,256,256]{1,2,0:T(8,128)(2,1)S(1)} %pad_maximum_fusion), channel_id=1, source_target_pairs={{0,1},{1,2},{2,3},{3,4},{4,5},{5,6},{6,7},{7,8},{8,9},{9,10},{10,1... | collective-permute-start | bytes 786440 | tf_op jit(solution)/shard_map/ppermute | solution.py:21
  75.0 26.2 %collective-permute-start.2 = (bf16[2,256,256]{1,2,0:T(8,128)(2,1)S(1)}, bf16[2,256,256]{1,2,0:T(8,128)(2,1)S(1)}, u32[]{:S(2)}, u32[]{:S(2)}) collective-permute-start(bf16[2,256,256]{1,2,0:T(8,128)(2,1)S(1)} %pad_maximum_fusion), channel_id=1, source_target_pairs={{0,2},{1,3},{2,4},{3,5},{4,6},{5,7},{6,8},{7,9},{8,10},{9,11},{10,... | collective-permute-start | bytes 786440 | tf_op jit(solution)/shard_map/ppermute | solution.py:21
  79.6 40.3 %collective-permute-start.3 = (bf16[2,256,256]{1,2,0:T(8,128)(2,1)S(1)}, bf16[2,256,256]{1,2,0:T(8,128)(2,1)S(1)}, u32[]{:S(2)}, u32[]{:S(2)}) collective-permute-start(bf16[2,256,256]{1,2,0:T(8,128)(2,1)S(1)} %pad_maximum_fusion), channel_id=1, source_target_pairs={{0,3},{1,4},{2,5},{3,6},{4,7},{5,8},{6,9},{7,10},{8,11},{9,12},{10... | collective-permute-start | bytes 786440 | tf_op jit(solution)/shard_map/ppermute | solution.py:21
  84.9 38.5 %collective-permute-start.4 = (bf16[2,256,256]{1,2,0:T(8,128)(2,1)S(1)}, bf16[2,256,256]{1,2,0:T(8,128)(2,1)S(1)}, u32[]{:S(2)}, u32[]{:S(2)}) collective-permute-start(bf16[2,256,256]{1,2,0:T(8,128)(2,1)S(1)} %pad_maximum_fusion), channel_id=1, source_target_pairs={{0,4},{1,5},{2,6},{3,7},{4,8},{5,9},{6,10},{7,11},{8,12},{9,13},{1... | collective-permute-start | bytes 786440 | tf_op jit(solution)/shard_map/ppermute | solution.py:21
  90.3 34.4 %collective-permute-start.5 = (bf16[2,256,256]{1,2,0:T(8,128)(2,1)S(1)}, bf16[2,256,256]{1,2,0:T(8,128)(2,1)S(1)}, u32[]{:S(2)}, u32[]{:S(2)}) collective-permute-start(bf16[2,256,256]{1,2,0:T(8,128)(2,1)S(1)} %pad_maximum_fusion), channel_id=1, source_target_pairs={{0,5},{1,6},{2,7},{3,8},{4,9},{5,10},{6,11},{7,12},{8,13},{9,14},{... | collective-permute-start | bytes 786440 | tf_op jit(solution)/shard_map/ppermute | solution.py:21
  95.1 35.2 %collective-permute-start.6 = (bf16[2,256,256]{1,2,0:T(8,128)(2,1)S(1)}, bf16[2,256,256]{1,2,0:T(8,128)(2,1)S(1)}, u32[]{:S(2)}, u32[]{:S(2)}) collective-permute-start(bf16[2,256,256]{1,2,0:T(8,128)(2,1)S(1)} %pad_maximum_fusion), channel_id=1, source_target_pairs={{0,6},{1,7},{2,8},{3,9},{4,10},{5,11},{6,12},{7,13},{8,14},{9,15},... | collective-permute-start | bytes 786440 | tf_op jit(solution)/shard_map/ppermute | solution.py:21
  101.2 45.6 %collective-permute-start.7 = (bf16[2,256,256]{1,2,0:T(8,128)(2,1)S(1)}, bf16[2,256,256]{1,2,0:T(8,128)(2,1)S(1)}, u32[]{:S(2)}, u32[]{:S(2)}) collective-permute-start(bf16[2,256,256]{1,2,0:T(8,128)(2,1)S(1)} %pad_maximum_fusion), channel_id=1, source_target_pairs={{0,7},{1,8},{2,9},{3,10},{4,11},{5,12},{6,13},{7,14},{8,15},{9,16}... | collective-permute-start | bytes 786440 | tf_op jit(solution)/shard_map/ppermute | solution.py:21
  120.0 29.6 %collective-permute-start.8 = (bf16[2,256,256]{1,2,0:T(8,128)(2,1)S(1)}, bf16[2,256,256]{1,2,0:T(8,128)(2,1)S(1)}, u32[]{:S(2)}, u32[]{:S(2)}) collective-permute-start(bf16[2,256,256]{1,2,0:T(8,128)(2,1)S(1)} %pad_maximum_fusion), channel_id=1, source_target_pairs={{0,8},{1,9},{2,10},{3,11},{4,12},{5,13},{6,14},{7,15},{8,16},{9,17... | collective-permute-start | bytes 786440 | tf_op jit(solution)/shard_map/ppermute | solution.py:21
  123.4 30.7 %collective-permute-start.9 = (bf16[2,256,256]{1,2,0:T(8,128)(2,1)S(1)}, bf16[2,256,256]{1,2,0:T(8,128)(2,1)S(1)}, u32[]{:S(2)}, u32[]{:S(2)}) collective-permute-start(bf16[2,256,256]{1,2,0:T(8,128)(2,1)S(1)} %pad_maximum_fusion), channel_id=1, source_target_pairs={{0,9},{1,10},{2,11},{3,12},{4,13},{5,14},{6,15},{7,16},{8,17},{9,1... | collective-permute-start | bytes 786440 | tf_op jit(solution)/shard_map/ppermute | solution.py:21
  124.8 34.7 %collective-permute-start.10 = (bf16[2,256,256]{1,2,0:T(8,128)(2,1)S(1)}, bf16[2,256,256]{1,2,0:T(8,128)(2,1)S(1)}, u32[]{:S(2)}, u32[]{:S(2)}) collective-permute-start(bf16[2,256,256]{1,2,0:T(8,128)(2,1)S(1)} %pad_maximum_fusion), channel_id=1, source_target_pairs={{0,10},{1,11},{2,12},{3,13},{4,14},{5,15},{6,16},{7,17},{8,18},{9,... | collective-permute-start | bytes 786440 | tf_op jit(solution)/shard_map/ppermute | solution.py:21
  130.3 42.5 %collective-permute-start.11 = (bf16[2,256,256]{1,2,0:T(8,128)(2,1)S(1)}, bf16[2,256,256]{1,2,0:T(8,128)(2,1)S(1)}, u32[]{:S(2)}, u32[]{:S(2)}) collective-permute-start(bf16[2,256,256]{1,2,0:T(8,128)(2,1)S(1)} %pad_maximum_fusion), channel_id=1, source_target_pairs={{0,11},{1,12},{2,13},{3,14},{4,15},{5,16},{6,17},{7,18},{8,19},{9,... | collective-permute-start | bytes 786440 | tf_op jit(solution)/shard_map/ppermute | solution.py:21
  146.7 56.4 %collective-permute-start.12 = (bf16[2,256,256]{1,2,0:T(8,128)(2,1)S(1)}, bf16[2,256,256]{1,2,0:T(8,128)(2,1)S(1)}, u32[]{:S(2)}, u32[]{:S(2)}) collective-permute-start(bf16[2,256,256]{1,2,0:T(8,128)(2,1)S(1)} %pad_maximum_fusion), channel_id=1, source_target_pairs={{0,12},{1,13},{2,14},{3,15},{4,16},{5,17},{6,18},{7,19},{8,20},{9,... | collective-permute-start | bytes 786440 | tf_op jit(solution)/shard_map/ppermute | solution.py:21
  149.6 53.6 %collective-permute-start.13 = (bf16[2,256,256]{1,2,0:T(8,128)(2,1)S(1)}, bf16[2,256,256]{1,2,0:T(8,128)(2,1)S(1)}, u32[]{:S(2)}, u32[]{:S(2)}) collective-permute-start(bf16[2,256,256]{1,2,0:T(8,128)(2,1)S(1)} %pad_maximum_fusion), channel_id=1, source_target_pairs={{0,13},{1,14},{2,15},{3,16},{4,17},{5,18},{6,19},{7,20},{8,21},{9,... | collective-permute-start | bytes 786440 | tf_op jit(solution)/shard_map/ppermute | solution.py:21
  154.1 49.1 %collective-permute-start.14 = (bf16[2,256,256]{1,2,0:T(8,128)(2,1)S(1)}, bf16[2,256,256]{1,2,0:T(8,128)(2,1)S(1)}, u32[]{:S(2)}, u32[]{:S(2)}) collective-permute-start(bf16[2,256,256]{1,2,0:T(8,128)(2,1)S(1)} %pad_maximum_fusion), channel_id=1, source_target_pairs={{0,14},{1,15},{2,16},{3,17},{4,18},{5,19},{6,20},{7,21},{8,22},{9,... | collective-permute-start | bytes 786440 | tf_op jit(solution)/shard_map/ppermute | solution.py:21
  159.5 51.4 %collective-permute-start.15 = (bf16[2,256,256]{1,2,0:T(8,128)(2,1)S(1)}, bf16[2,256,256]{1,2,0:T(8,128)(2,1)S(1)}, u32[]{:S(2)}, u32[]{:S(2)}) collective-permute-start(bf16[2,256,256]{1,2,0:T(8,128)(2,1)S(1)} %pad_maximum_fusion), channel_id=1, source_target_pairs={{0,15},{1,16},{2,17},{3,18},{4,19},{5,20},{6,21},{7,22},{8,23},{9,... | collective-permute-start | bytes 786440 | tf_op jit(solution)/shard_map/ppermute | solution.py:21
  172.8 43.8 %collective-permute-start.16 = (bf16[2,256,256]{1,2,0:T(8,128)(2,1)S(1)}, bf16[2,256,256]{1,2,0:T(8,128)(2,1)S(1)}, u32[]{:S(2)}, u32[]{:S(2)}) collective-permute-start(bf16[2,256,256]{1,2,0:T(8,128)(2,1)S(1)} %pad_maximum_fusion), channel_id=1, source_target_pairs={{0,16},{1,17},{2,18},{3,19},{4,20},{5,21},{6,22},{7,23},{8,24},{9,... | collective-permute-start | bytes 786440 | tf_op jit(solution)/shard_map/ppermute | solution.py:21
  230.4 2.0 copy-start.3
  239.6 0.7 copy-start.11
  239.6 149.3 %copy-start.5 = (f32[2560]{0:T(1024)S(1)}, f32[2560]{0:T(1024)}, u32[]{:S(2)}) copy-start(f32[2560]{0:T(1024)} %param.18) | copy-start | bytes 30724
  239.6 150.4 %all-gather.5.cloned.1.call-start = ((), (), s32[]{:S(2)}) async-start(), calls=%async_computation.2 | async-start | bytes 6656000 | tf_op jit(solution)/shard_map/all_gather | solution.py:127
  241.0 148.9 %copy-start.4 = (bf16[2,128,256]{2,1,0:T(8,128)(2,1)}, bf16[2,128,256]{2,1,0:T(8,128)(2,1)S(1)}, u32[]{:S(2)}) copy-start(bf16[2,128,256]{2,1,0:T(8,128)(2,1)S(1)} %scatter_fusion) | copy-start | bytes 393220
  386.7 2.5 copy-start.1
  390.0 4.2 %copy-start.2 = (f32[256,2560]{1,0:T(8,128)S(1)}, f32[256,2560]{1,0:T(8,128)}, u32[]{:S(2)}) copy-start(f32[256,2560]{1,0:T(8,128)} %all-reduce.2.cloned.1.call-done) | copy-start | bytes 7864324
  390.0 4.2 %copy-start.10 = (f32[2560]{0:T(1024)S(1)}, f32[2560]{0:T(1024)}, u32[]{:S(2)}) copy-start(f32[2560]{0:T(1024)} %param.19) | copy-start | bytes 30724
Sparse Core Ops, SparseCore 0:
  10.9 49.6 all-gather.2
  239.8 146.9 all-reduce.1
Sparse Core Ops, SparseCore 1:
  243.4 133.3 all-gather.4
where the time goes:
time: 406 us; the launch traced here: 405 us
  waiting for transfers between devices  214 us (53%)
  starting transfers between devices  132 us (33%)
  local copies, waits for them, and re-layouts  19.8 us (5%)
  between operations  16.2 us (4%)
  matrix products  14.9 us (4%)
  other arithmetic  8.28 us (2%)
    psum x1, waiting for transfers between devices, local(): attended = lax.psum(head_terms, ('section', 'tensor'))  146 us
    ppermute x16, starting transfers between devices, shifted(): return lax.ppermute(block, axis, route)  130 us
    all_gather x1, waiting for transfers between devices, local(): features = lax.all_gather(tokens, ('section', 'tensor'), axis=1, tiled=True)  49.9 us
    ppermute x16, waiting for transfers between devices, shifted(): return lax.ppermute(block, axis, route)  13.3 us
  transfers between devices with their start and end apart: 20, of which 5 were waited for; matrix products, arithmetic and copies ran while one was open for 2% of the time, Pallas kernels for 0%

commit v1 on v0

--- a/solution.py
+++ b/solution.py
@@ -67,7 +67,12 @@
     halfway = head_width // 2
     unit_count = w_gateup.shape[2]
     span_blocks = min(REACH, lax.axis_size("seq") // 2)
-    features = lax.all_gather(tokens, ("section", "tensor"), axis=1, tiled=True)
+    features = jnp.concatenate(
+        lax.all_to_all(
+            jnp.stack([tokens] * lax.axis_size(("section", "tensor"))), ("section", "tensor"), 0, 0
+        ),
+        axis=1,
+    )
     first_row = lax.axis_index("seq") * row_count
     prompt_ends = jnp.cumsum(prompt_lengths)
     prompt_starts = prompt_ends - prompt_lengths

time: 406 us -> 383 us (0.943)
  waiting for transfers between devices: 214 us -> 199 us
  starting transfers between devices: 132 us -> 119 us
  other arithmetic: 8.28 us -> 12.5 us
    all_gather x1 -> x0, waiting for transfers between devices: 49.9 us -> none  [local(): features = lax.all_gather(tokens, ('section', 'tensor'), axis=1, tiled=True)]
    ppermute x16, waiting for transfers between devices: 13.3 us -> 41.3 us  [shifted(): return lax.ppermute(block, axis, route)]
    ppermute x16, starting transfers between devices: 130 us -> 110 us  [shifted(): return lax.ppermute(block, axis, route)]
    all_to_all x0 -> x1, waiting for transfers between devices: none -> 16.3 us  [local(): lax.all_to_all(jnp.stack([tokens] * lax.axis_size(('section', 'tensor')))...]
    psum x1, waiting for transfers between devices: 146 us -> 138 us  [local(): attended = lax.psum(head_terms, ('section', 'tensor'))]
    all_to_all x0 -> x1, starting transfers between devices: none -> 6.11 us  [local(): lax.all_to_all(jnp.stack([tokens] * lax.axis_size(('section', 'tensor')))...]
  transfers between devices with their start and end apart: 20 -> 20, of which waited for: 5 -> 7; matrix products, arithmetic and copies ran while one was open for 2% -> 3% of each run, Pallas kernels for 0% -> 0%
where the time goes in v1:
time: 383 us; the launch traced here: 382 us
  waiting for transfers between devices  199 us (52%)
  starting transfers between devices  119 us (31%)
  local copies, waits for them, and re-layouts  22.2 us (6%)
  between operations  16.2 us (4%)
  matrix products  12.6 us (3%)
  other arithmetic  12.5 us (3%)
    psum x1, waiting for transfers between devices, local(): attended = lax.psum(head_terms, ('section', 'tensor'))  138 us
    ppermute x16, starting transfers between devices, shifted(): return lax.ppermute(block, axis, route)  110 us
    ppermute x16, waiting for transfers between devices, shifted(): return lax.ppermute(block, axis, route)  41.3 us
    all_to_all x1, waiting for transfers between devices, local(): lax.all_to_all(jnp.stack([tokens] * lax.axis_size(('section', 'tensor')))...  16.3 us
    unnamed x56, local copies, waits for them, and re-layouts  7.89 us
  transfers between devices with their start and end apart: 20, of which 7 were waited for; matrix products, arithmetic and copies ran while one was open for 3% of the time, Pallas kernels for 0%

profile of v1, /device:TPU:8, one launch (start us, length us, event | category | flops | bytes accessed | tf_op | source)
XLA Modules:
  0.0 381.6 jit_solution(7420378365079664568)
XLA Ops:
  8.0 2.2 stack.72
  10.2 6.1 %all-to-all-start = ((bf16[8,256,320]{1,2,0:T(8,128)(2,1)}), bf16[8,256,320]{1,2,0:T(8,128)(2,1)S(1)}, u32[]{:S(2)}, u32[]{:S(2)}) async-start(bf16[8,256,320]{1,2,0:T(8,128)(2,1)} %stack.72), calls=%async_computation | async-start | bytes 2621440 | tf_op jit(solution)/shard_map/all_to_all | solution.py:71
  17.0 0.6 compare_select_fusion
  17.6 16.3 %all-to-all-done = bf16[8,256,320]{1,2,0:T(8,128)(2,1)S(1)} async-done(((bf16[8,256,320]{1,2,0:T(8,128)(2,1)}), bf16[8,256,320]{1,2,0:T(8,128)(2,1)S(1)}, u32[]{:S(2)}, u32[]{:S(2)}) %all-to-all-start) | async-done | bytes 1310752 | tf_op jit(solution)/shard_map/all_to_all | solution.py:71
  33.9 0.4 multiply_reduce_fusion.2
  34.3 1.9 multiply_convert_fusion.1
  36.2 0.6 convolution_convert_fusion
  36.9 2.9 collective-permute-start
  39.8 0.7 multiply_reduce_fusion.3
  40.6 3.4 collective-permute-done
  44.3 1.2 broadcast_select_fusion.2
  45.6 1.9 collective-permute-start.1
  47.5 1.2 fusion.28
  48.7 6.1 %collective-permute-start.2 = (bf16[2,256,256]{1,2,0:T(8,128)(2,1)S(1)}, bf16[2,256,256]{1,2,0:T(8,128)(2,1)S(1)}, u32[]{:S(2)}, u32[]{:S(2)}) collective-permute-start(bf16[2,256,256]{1,2,0:T(8,128)(2,1)S(1)} %pad_maximum_fusion), channel_id=1, source_target_pairs={{0,2},{1,3},{2,4},{3,5},{4,6},{5,7},{6,8},{7,9},{8,10},{9,11},{10,... | collective-permute-start | bytes 786440 | tf_op jit(solution)/shard_map/ppermute | solution.py:21
  54.8 8.2 %collective-permute-start.3 = (bf16[2,256,256]{1,2,0:T(8,128)(2,1)S(1)}, bf16[2,256,256]{1,2,0:T(8,128)(2,1)S(1)}, u32[]{:S(2)}, u32[]{:S(2)}) collective-permute-start(bf16[2,256,256]{1,2,0:T(8,128)(2,1)S(1)} %pad_maximum_fusion), channel_id=1, source_target_pairs={{0,3},{1,4},{2,5},{3,6},{4,7},{5,8},{6,9},{7,10},{8,11},{9,12},{10... | collective-permute-start | bytes 786440 | tf_op jit(solution)/shard_map/ppermute | solution.py:21
  63.0 2.5 collective-permute-start.4
  65.6 7.7 %collective-permute-start.5 = (bf16[2,256,256]{1,2,0:T(8,128)(2,1)S(1)}, bf16[2,256,256]{1,2,0:T(8,128)(2,1)S(1)}, u32[]{:S(2)}, u32[]{:S(2)}) collective-permute-start(bf16[2,256,256]{1,2,0:T(8,128)(2,1)S(1)} %pad_maximum_fusion), channel_id=1, source_target_pairs={{0,5},{1,6},{2,7},{3,8},{4,9},{5,10},{6,11},{7,12},{8,13},{9,14},{... | collective-permute-start | bytes 786440 | tf_op jit(solution)/shard_map/ppermute | solution.py:21
  73.3 4.7 %collective-permute-start.6 = (bf16[2,256,256]{1,2,0:T(8,128)(2,1)S(1)}, bf16[2,256,256]{1,2,0:T(8,128)(2,1)S(1)}, u32[]{:S(2)}, u32[]{:S(2)}) collective-permute-start(bf16[2,256,256]{1,2,0:T(8,128)(2,1)S(1)} %pad_maximum_fusion), channel_id=1, source_target_pairs={{0,6},{1,7},{2,8},{3,9},{4,10},{5,11},{6,12},{7,13},{8,14},{9,15},... | collective-permute-start | bytes 786440 | tf_op jit(solution)/shard_map/ppermute | solution.py:21
  78.0 19.3 %collective-permute-start.7 = (bf16[2,256,256]{1,2,0:T(8,128)(2,1)S(1)}, bf16[2,256,256]{1,2,0:T(8,128)(2,1)S(1)}, u32[]{:S(2)}, u32[]{:S(2)}) collective-permute-start(bf16[2,256,256]{1,2,0:T(8,128)(2,1)S(1)} %pad_maximum_fusion), channel_id=1, source_target_pairs={{0,7},{1,8},{2,9},{3,10},{4,11},{5,12},{6,13},{7,14},{8,15},{9,16}... | collective-permute-start | bytes 786440 | tf_op jit(solution)/shard_map/ppermute | solution.py:21
  97.3 3.5 collective-permute-start.8
  100.8 1.3 collective-permute-start.9
  102.2 3.7 collective-permute-start.10
  105.9 19.1 %collective-permute-start.11 = (bf16[2,256,256]{1,2,0:T(8,128)(2,1)S(1)}, bf16[2,256,256]{1,2,0:T(8,128)(2,1)S(1)}, u32[]{:S(2)}, u32[]{:S(2)}) collective-permute-start(bf16[2,256,256]{1,2,0:T(8,128)(2,1)S(1)} %pad_maximum_fusion), channel_id=1, source_target_pairs={{0,11},{1,12},{2,13},{3,14},{4,15},{5,16},{6,17},{7,18},{8,19},{9,... | collective-permute-start | bytes 786440 | tf_op jit(solution)/shard_map/ppermute | solution.py:21
  125.0 3.2 collective-permute-start.12
  128.2 4.2 %collective-permute-start.13 = (bf16[2,256,256]{1,2,0:T(8,128)(2,1)S(1)}, bf16[2,256,256]{1,2,0:T(8,128)(2,1)S(1)}, u32[]{:S(2)}, u32[]{:S(2)}) collective-permute-start(bf16[2,256,256]{1,2,0:T(8,128)(2,1)S(1)} %pad_maximum_fusion), channel_id=1, source_target_pairs={{0,13},{1,14},{2,15},{3,16},{4,17},{5,18},{6,19},{7,20},{8,21},{9,... | collective-permute-start | bytes 786440 | tf_op jit(solution)/shard_map/ppermute | solution.py:21
  132.5 2.3 collective-permute-start.14
  134.9 10.5 %collective-permute-start.15 = (bf16[2,256,256]{1,2,0:T(8,128)(2,1)S(1)}, bf16[2,256,256]{1,2,0:T(8,128)(2,1)S(1)}, u32[]{:S(2)}, u32[]{:S(2)}) collective-permute-start(bf16[2,256,256]{1,2,0:T(8,128)(2,1)S(1)} %pad_maximum_fusion), channel_id=1, source_target_pairs={{0,15},{1,16},{2,17},{3,18},{4,19},{5,20},{6,21},{7,22},{8,23},{9,... | collective-permute-start | bytes 786440 | tf_op jit(solution)/shard_map/ppermute | solution.py:21
  145.4 11.5 %collective-permute-start.16 = (bf16[2,256,256]{1,2,0:T(8,128)(2,1)S(1)}, bf16[2,256,256]{1,2,0:T(8,128)(2,1)S(1)}, u32[]{:S(2)}, u32[]{:S(2)}) collective-permute-start(bf16[2,256,256]{1,2,0:T(8,128)(2,1)S(1)} %pad_maximum_fusion), channel_id=1, source_target_pairs={{0,16},{1,17},{2,18},{3,19},{4,20},{5,21},{6,22},{7,23},{8,24},{9,... | collective-permute-start | bytes 786440 | tf_op jit(solution)/shard_map/ppermute | solution.py:21
  157.0 4.3 %collective-permute-done.13 = bf16[2,256,256]{1,2,0:T(8,128)(2,1)S(1)} collective-permute-done((bf16[2,256,256]{1,2,0:T(8,128)(2,1)S(1)}, bf16[2,256,256]{1,2,0:T(8,128)(2,1)S(1)}, u32[]{:S(2)}, u32[]{:S(2)}) %collective-permute-start.13) | collective-permute-done | bytes 262176 | tf_op jit(solution)/shard_map/ppermute | solution.py:21
  161.3 17.0 %collective-permute-done.14 = bf16[2,256,256]{1,2,0:T(8,128)(2,1)S(1)} collective-permute-done((bf16[2,256,256]{1,2,0:T(8,128)(2,1)S(1)}, bf16[2,256,256]{1,2,0:T(8,128)(2,1)S(1)}, u32[]{:S(2)}, u32[]{:S(2)}) %collective-permute-start.14) | collective-permute-done | bytes 262176 | tf_op jit(solution)/shard_map/ppermute | solution.py:21
  178.3 14.4 %collective-permute-done.15 = bf16[2,256,256]{1,2,0:T(8,128)(2,1)S(1)} collective-permute-done((bf16[2,256,256]{1,2,0:T(8,128)(2,1)S(1)}, bf16[2,256,256]{1,2,0:T(8,128)(2,1)S(1)}, u32[]{:S(2)}, u32[]{:S(2)}) %collective-permute-start.15) | collective-permute-done | bytes 262176 | tf_op jit(solution)/shard_map/ppermute | solution.py:21
  192.8 5.6 %collective-permute-done.16 = bf16[2,256,256]{1,2,0:T(8,128)(2,1)S(1)} collective-permute-done((bf16[2,256,256]{1,2,0:T(8,128)(2,1)S(1)}, bf16[2,256,256]{1,2,0:T(8,128)(2,1)S(1)}, u32[]{:S(2)}, u32[]{:S(2)}) %collective-permute-start.16) | collective-permute-done | bytes 262176 | tf_op jit(solution)/shard_map/ppermute | solution.py:21
  198.4 1.6 fusion.41
  200.0 4.1 %copy.24 = bf16[17,1,256,256]{3,2,0,1:T(8,128)(2,1)} copy(bf16[17,1,256,256]{2,3,1,0:T(8,128)(2,1)} %get-tuple-element.7) | data formatting | bytes 4456448 | tf_op jit(solution)/shard_map/slice | solution.py:107
  204.1 2.4 copy.25
  206.6 3.4 fusion.44
  210.0 2.3 copy-done.4
  212.2 0.7 fusion.1
  213.2 5.7 %fusion.7 = f32[256,2560]{1,0:T(8,128)} fusion(bf16[256,2560]{1,0:T(8,128)(2,1)S(1)} %copy-done, bf16[4352,256]{1,0:T(8,128)(2,1)S(1)} %bitcast.61, f32[256,4352]{1,0:T(8,128)} %copy-done.4, f32[256]{0:T(256)S(1)} %fusion.1, f32[256]{0:T(256)S(1)} %get-tuple-element.19), kind=kOutput, calls=%fused_computation.18 | convolution fusion | flops 909377536 | bytes 10618880 | tf_op jit(solution)/shard_map/dot_general | solution.py:128
  219.9 3.2 copy.26
  223.2 0.6 scatter_fusion
  223.9 137.8 %all-reduce.2.cloned.1.call-done = f32[256,2560]{1,0:T(8,128)} async-done(((f32[256,2560]{1,0:T(8,128)}), f32[256,2560]{1,0:T(8,128)}) %all-reduce.2.cloned.1.call-update) | async-done | bytes 2621456 | tf_op jit(solution)/shard_map/psum | solution.py:129
  361.7 2.1 multiply_reduce_fusion.1
  363.8 0.4 copy-done.1
  364.2 2.4 multiply_reduce_fusion
  366.7 4.1 %copy.29 = bf16[320,8,2,640]{3,1,2,0:T(8,128)(2,1)S(1)} copy(bf16[320,8,2,640]{3,2,1,0:T(2,128)(2,1)} %bitcast.60) | data formatting | bytes 13107200
  371.1 2.1 fusion.3
  373.2 1.0 fusion.16
  (100 shorter events, 2.9 us)
Async XLA Ops:
  8.0 205.0 %copy-start = (bf16[256,2560]{1,0:T(8,128)(2,1)S(1)}, bf16[256,2560]{1,0:T(8,128)(2,1)}, u32[]{:S(2)}) copy-start(bf16[256,2560]{1,0:T(8,128)(2,1)} %param.15) | copy-start | bytes 3932164
  8.0 8.4 %copy-start.18 = (s32[8]{0:T(128)S(1)}, s32[8]{0:T(128)}, u32[]{:S(2)}) copy-start(s32[8]{0:T(128)} %param.22) | copy-start | bytes 100
  8.0 26.3 %copy-start.12 = (f32[2560]{0:T(1024)S(1)}, f32[2560]{0:T(1024)}, u32[]{:S(2)}) copy-start(f32[2560]{0:T(1024)} %param.17) | copy-start | bytes 30724
  10.2 23.7 %all-to-all-start = ((bf16[8,256,320]{1,2,0:T(8,128)(2,1)}), bf16[8,256,320]{1,2,0:T(8,128)(2,1)S(1)}, u32[]{:S(2)}, u32[]{:S(2)}) async-start(bf16[8,256,320]{1,2,0:T(8,128)(2,1)} %stack.72), calls=%async_computation | async-start | bytes 2621440 | tf_op jit(solution)/shard_map/all_to_all | solution.py:71
  16.3 345.4 %all-reduce.2.cloned.1.call-start = ((), (), s32[]{:S(2)}) async-start(), calls=%async_computation.1 | async-start | bytes 5242880 | tf_op jit(solution)/shard_map/psum | solution.py:129
  16.6 19.6 %copy-start.10 = (s32[4352]{0:T(1024)}, s32[4352]{0:T(1024)S(1)}, u32[]{:S(2)}) copy-start(s32[4352]{0:T(1024)S(1)} %add.111) | copy-start | bytes 52228
  34.3 1.9 copy-start.16
  36.2 3.6 copy-start.17
  36.2 4.3 %copy-start.14 = (f32[256]{0:T(256)S(1)}, f32[256]{0:T(256)}, u32[]{:S(2)}) copy-start(f32[256]{0:T(256)} %param.20) | copy-start | bytes 3076
  36.9 7.4 %copy-start.7 = (bf16[256,256]{0,1:T(8,128)(2,1)}, bf16[256,256]{0,1:T(8,128)(2,1)S(1)}, u32[]{:S(2)}) copy-start(bf16[256,256]{0,1:T(8,128)(2,1)S(1)} %convolution_convert_fusion) | copy-start | bytes 393220
  36.9 7.3 %copy-start.15 = (f32[256]{0:T(256)S(1)}, f32[256]{0:T(256)}, u32[]{:S(2)}) copy-start(f32[256]{0:T(256)} %param.21) | copy-start | bytes 3076
  36.9 7.1 %collective-permute-start = (bf16[256,256]{0,1:T(8,128)(2,1)S(1)}, bf16[256,256]{0,1:T(8,128)(2,1)S(1)}, u32[]{:S(2)}, u32[]{:S(2)}) collective-permute-start(bf16[256,256]{0,1:T(8,128)(2,1)S(1)} %convolution_convert_fusion), channel_id=1, source_target_pairs={{0,64},{64,0},{128,192},{192,128},{1,65},{65,1},{129,193},{193,129... | collective-permute-start | bytes 393224 | tf_op jit(solution)/shard_map/ppermute | solution.py:15
  45.6 27.7 %collective-permute-start.1 = (bf16[2,256,256]{1,2,0:T(8,128)(2,1)S(1)}, bf16[2,256,256]{1,2,0:T(8,128)(2,1)S(1)}, u32[]{:S(2)}, u32[]{:S(2)}) collective-permute-start(bf16[2,256,256]{1,2,0:T(8,128)(2,1)S(1)} %pad_maximum_fusion), channel_id=1, source_target_pairs={{0,1},{1,2},{2,3},{3,4},{4,5},{5,6},{6,7},{7,8},{8,9},{9,10},{10,1... | collective-permute-start | bytes 786440 | tf_op jit(solution)/shard_map/ppermute | solution.py:21
  48.7 29.3 %collective-permute-start.2 = (bf16[2,256,256]{1,2,0:T(8,128)(2,1)S(1)}, bf16[2,256,256]{1,2,0:T(8,128)(2,1)S(1)}, u32[]{:S(2)}, u32[]{:S(2)}) collective-permute-start(bf16[2,256,256]{1,2,0:T(8,128)(2,1)S(1)} %pad_maximum_fusion), channel_id=1, source_target_pairs={{0,2},{1,3},{2,4},{3,5},{4,6},{5,7},{6,8},{7,9},{8,10},{9,11},{10,... | collective-permute-start | bytes 786440 | tf_op jit(solution)/shard_map/ppermute | solution.py:21
  54.8 42.5 %collective-permute-start.3 = (bf16[2,256,256]{1,2,0:T(8,128)(2,1)S(1)}, bf16[2,256,256]{1,2,0:T(8,128)(2,1)S(1)}, u32[]{:S(2)}, u32[]{:S(2)}) collective-permute-start(bf16[2,256,256]{1,2,0:T(8,128)(2,1)S(1)} %pad_maximum_fusion), channel_id=1, source_target_pairs={{0,3},{1,4},{2,5},{3,6},{4,7},{5,8},{6,9},{7,10},{8,11},{9,12},{10... | collective-permute-start | bytes 786440 | tf_op jit(solution)/shard_map/ppermute | solution.py:21
  63.0 37.8 %collective-permute-start.4 = (bf16[2,256,256]{1,2,0:T(8,128)(2,1)S(1)}, bf16[2,256,256]{1,2,0:T(8,128)(2,1)S(1)}, u32[]{:S(2)}, u32[]{:S(2)}) collective-permute-start(bf16[2,256,256]{1,2,0:T(8,128)(2,1)S(1)} %pad_maximum_fusion), channel_id=1, source_target_pairs={{0,4},{1,5},{2,6},{3,7},{4,8},{5,9},{6,10},{7,11},{8,12},{9,13},{1... | collective-permute-start | bytes 786440 | tf_op jit(solution)/shard_map/ppermute | solution.py:21
  65.6 36.6 %collective-permute-start.5 = (bf16[2,256,256]{1,2,0:T(8,128)(2,1)S(1)}, bf16[2,256,256]{1,2,0:T(8,128)(2,1)S(1)}, u32[]{:S(2)}, u32[]{:S(2)}) collective-permute-start(bf16[2,256,256]{1,2,0:T(8,128)(2,1)S(1)} %pad_maximum_fusion), channel_id=1, source_target_pairs={{0,5},{1,6},{2,7},{3,8},{4,9},{5,10},{6,11},{7,12},{8,13},{9,14},{... | collective-permute-start | bytes 786440 | tf_op jit(solution)/shard_map/ppermute | solution.py:21
  73.3 32.6 %collective-permute-start.6 = (bf16[2,256,256]{1,2,0:T(8,128)(2,1)S(1)}, bf16[2,256,256]{1,2,0:T(8,128)(2,1)S(1)}, u32[]{:S(2)}, u32[]{:S(2)}) collective-permute-start(bf16[2,256,256]{1,2,0:T(8,128)(2,1)S(1)} %pad_maximum_fusion), channel_id=1, source_target_pairs={{0,6},{1,7},{2,8},{3,9},{4,10},{5,11},{6,12},{7,13},{8,14},{9,15},... | collective-permute-start | bytes 786440 | tf_op jit(solution)/shard_map/ppermute | solution.py:21
  78.0 47.0 %collective-permute-start.7 = (bf16[2,256,256]{1,2,0:T(8,128)(2,1)S(1)}, bf16[2,256,256]{1,2,0:T(8,128)(2,1)S(1)}, u32[]{:S(2)}, u32[]{:S(2)}) collective-permute-start(bf16[2,256,256]{1,2,0:T(8,128)(2,1)S(1)} %pad_maximum_fusion), channel_id=1, source_target_pairs={{0,7},{1,8},{2,9},{3,10},{4,11},{5,12},{6,13},{7,14},{8,15},{9,16}... | collective-permute-start | bytes 786440 | tf_op jit(solution)/shard_map/ppermute | solution.py:21
  97.3 30.9 %collective-permute-start.8 = (bf16[2,256,256]{1,2,0:T(8,128)(2,1)S(1)}, bf16[2,256,256]{1,2,0:T(8,128)(2,1)S(1)}, u32[]{:S(2)}, u32[]{:S(2)}) collective-permute-start(bf16[2,256,256]{1,2,0:T(8,128)(2,1)S(1)} %pad_maximum_fusion), channel_id=1, source_target_pairs={{0,8},{1,9},{2,10},{3,11},{4,12},{5,13},{6,14},{7,15},{8,16},{9,17... | collective-permute-start | bytes 786440 | tf_op jit(solution)/shard_map/ppermute | solution.py:21
  100.8 31.7 %collective-permute-start.9 = (bf16[2,256,256]{1,2,0:T(8,128)(2,1)S(1)}, bf16[2,256,256]{1,2,0:T(8,128)(2,1)S(1)}, u32[]{:S(2)}, u32[]{:S(2)}) collective-permute-start(bf16[2,256,256]{1,2,0:T(8,128)(2,1)S(1)} %pad_maximum_fusion), channel_id=1, source_target_pairs={{0,9},{1,10},{2,11},{3,12},{4,13},{5,14},{6,15},{7,16},{8,17},{9,1... | collective-permute-start | bytes 786440 | tf_op jit(solution)/shard_map/ppermute | solution.py:21
  102.2 32.7 %collective-permute-start.10 = (bf16[2,256,256]{1,2,0:T(8,128)(2,1)S(1)}, bf16[2,256,256]{1,2,0:T(8,128)(2,1)S(1)}, u32[]{:S(2)}, u32[]{:S(2)}) collective-permute-start(bf16[2,256,256]{1,2,0:T(8,128)(2,1)S(1)} %pad_maximum_fusion), channel_id=1, source_target_pairs={{0,10},{1,11},{2,12},{3,13},{4,14},{5,15},{6,16},{7,17},{8,18},{9,... | collective-permute-start | bytes 786440 | tf_op jit(solution)/shard_map/ppermute | solution.py:21
  105.9 39.5 %collective-permute-start.11 = (bf16[2,256,256]{1,2,0:T(8,128)(2,1)S(1)}, bf16[2,256,256]{1,2,0:T(8,128)(2,1)S(1)}, u32[]{:S(2)}, u32[]{:S(2)}) collective-permute-start(bf16[2,256,256]{1,2,0:T(8,128)(2,1)S(1)} %pad_maximum_fusion), channel_id=1, source_target_pairs={{0,11},{1,12},{2,13},{3,14},{4,15},{5,16},{6,17},{7,18},{8,19},{9,... | collective-permute-start | bytes 786440 | tf_op jit(solution)/shard_map/ppermute | solution.py:21
  125.0 32.0 %collective-permute-start.12 = (bf16[2,256,256]{1,2,0:T(8,128)(2,1)S(1)}, bf16[2,256,256]{1,2,0:T(8,128)(2,1)S(1)}, u32[]{:S(2)}, u32[]{:S(2)}) collective-permute-start(bf16[2,256,256]{1,2,0:T(8,128)(2,1)S(1)} %pad_maximum_fusion), channel_id=1, source_target_pairs={{0,12},{1,13},{2,14},{3,15},{4,16},{5,17},{6,18},{7,19},{8,20},{9,... | collective-permute-start | bytes 786440 | tf_op jit(solution)/shard_map/ppermute | solution.py:21
  128.2 33.0 %collective-permute-start.13 = (bf16[2,256,256]{1,2,0:T(8,128)(2,1)S(1)}, bf16[2,256,256]{1,2,0:T(8,128)(2,1)S(1)}, u32[]{:S(2)}, u32[]{:S(2)}) collective-permute-start(bf16[2,256,256]{1,2,0:T(8,128)(2,1)S(1)} %pad_maximum_fusion), channel_id=1, source_target_pairs={{0,13},{1,14},{2,15},{3,16},{4,17},{5,18},{6,19},{7,20},{8,21},{9,... | collective-permute-start | bytes 786440 | tf_op jit(solution)/shard_map/ppermute | solution.py:21
  132.5 45.8 %collective-permute-start.14 = (bf16[2,256,256]{1,2,0:T(8,128)(2,1)S(1)}, bf16[2,256,256]{1,2,0:T(8,128)(2,1)S(1)}, u32[]{:S(2)}, u32[]{:S(2)}) collective-permute-start(bf16[2,256,256]{1,2,0:T(8,128)(2,1)S(1)} %pad_maximum_fusion), channel_id=1, source_target_pairs={{0,14},{1,15},{2,16},{3,17},{4,18},{5,19},{6,20},{7,21},{8,22},{9,... | collective-permute-start | bytes 786440 | tf_op jit(solution)/shard_map/ppermute | solution.py:21
  134.9 57.9 %collective-permute-start.15 = (bf16[2,256,256]{1,2,0:T(8,128)(2,1)S(1)}, bf16[2,256,256]{1,2,0:T(8,128)(2,1)S(1)}, u32[]{:S(2)}, u32[]{:S(2)}) collective-permute-start(bf16[2,256,256]{1,2,0:T(8,128)(2,1)S(1)} %pad_maximum_fusion), channel_id=1, source_target_pairs={{0,15},{1,16},{2,17},{3,18},{4,19},{5,20},{6,21},{7,22},{8,23},{9,... | collective-permute-start | bytes 786440 | tf_op jit(solution)/shard_map/ppermute | solution.py:21
  145.4 52.9 %collective-permute-start.16 = (bf16[2,256,256]{1,2,0:T(8,128)(2,1)S(1)}, bf16[2,256,256]{1,2,0:T(8,128)(2,1)S(1)}, u32[]{:S(2)}, u32[]{:S(2)}) collective-permute-start(bf16[2,256,256]{1,2,0:T(8,128)(2,1)S(1)} %pad_maximum_fusion), channel_id=1, source_target_pairs={{0,16},{1,17},{2,18},{3,19},{4,20},{5,21},{6,22},{7,23},{8,24},{9,... | collective-permute-start | bytes 786440 | tf_op jit(solution)/shard_map/ppermute | solution.py:21
  210.0 2.3 copy-start.4
  210.0 3.2 copy-start.5
  218.9 0.7 copy-start.19
  218.9 0.9 copy-start.8
  219.0 147.7 %all-gather.2.cloned.1.call-start = ((), (), s32[]{:S(2)}) async-start(), calls=%async_computation.2 | async-start | bytes 6656000 | tf_op jit(solution)/shard_map/all_gather | solution.py:132
  219.9 3.2 copy-start.9
  223.1 140.7 %copy-start.11 = (f32[2560]{0:T(1024)S(1)}, f32[2560]{0:T(1024)}, u32[]{:S(2)}) copy-start(f32[2560]{0:T(1024)} %param.18) | copy-start | bytes 30724
  223.9 142.7 %copy-start.6 = (bf16[2,128,256]{2,1,0:T(8,128)(2,1)}, bf16[2,128,256]{2,1,0:T(8,128)(2,1)S(1)}, u32[]{:S(2)}) copy-start(bf16[2,128,256]{2,1,0:T(8,128)(2,1)S(1)} %scatter_fusion) | copy-start | bytes 393220
  361.7 2.5 copy-start.1
  366.6 4.2 %copy-start.2 = (f32[256,2560]{1,0:T(8,128)S(1)}, f32[256,2560]{1,0:T(8,128)}, u32[]{:S(2)}) copy-start(f32[256,2560]{1,0:T(8,128)} %all-reduce.2.cloned.1.call-done) | copy-start | bytes 7864324
  366.7 4.4 %copy-start.3 = (f32[256,2560]{1,0:T(8,128)S(1)}, f32[256,2560]{1,0:T(8,128)}, u32[]{:S(2)}) copy-start(f32[256,2560]{1,0:T(8,128)} %copy.26) | copy-start | bytes 7864324
  366.7 4.4 %copy-start.13 = (f32[2560]{0:T(1024)S(1)}, f32[2560]{0:T(1024)}, u32[]{:S(2)}) copy-start(f32[2560]{0:T(1024)} %param.19) | copy-start | bytes 30724
Sparse Core Ops, SparseCore 0:
  219.1 142.5 all-reduce.1
Sparse Core Ops, SparseCore 1:
  222.7 129.3 all-gather.1
